TPU v7x, 512 devices: a whole 4x8x8 slice. The times are simulated.
512 devices in a mesh: op: 16 (over y_lo, z), bond: 32 (over y_hi, x, core).
Axes of the slice: x: 4, y: 8 (y_hi: 4, y_lo: 2; y = y_hi * 2 + y_lo), z: 8, core: 2. Of those that a mesh axis runs over, the one named last changes fastest.
Arguments:
- vectors: bfloat16 [2, 64, 256, 256], P(None, 'bond'), may hold values from -6 to 6
- left_ops: bfloat16 [128, 64, 256, 256], P('op', 'bond'), may hold values from -0.03125 to 0.03125
- right_ops: bfloat16 [128, 64, 256, 256], P('op', 'bond'), may hold values from -0.375 to 0.375
- block_sizes: int32 [64, 2], P('bond'), may hold values from 32 to 256, as said below
- term_shifts: int32 [128], P('op'), may hold values from -1 to 1
Outputs:
- sigma: float32 [2, 64, 256, 256], P(None, 'bond', 'op')
Inputs may be any that keep to these rules, and one draw needn't show every extreme that they name: `block_sizes`: some block has both live dimensions 256 and some other block both 256 // 8.
All inputs are finite; a program needn't handle non-finite values.
Results may differ from a plain program's by a relative error of at most 0.0029.
Values may be sent and summed in bfloat16 or wider, within the bound.
No kernel may reach another device: no remote copies, remote signals or barrier semaphores. Data moves between devices by JAX's collectives and lax.ppermute only.
A program may use at most 64 MiB of HBM per device.

v0:
```python
import jax
import jax.numpy as jnp
from jax import lax
from jax.sharding import PartitionSpec as P


def extended(cells, sides, width):
    for axis, dim in sides:
        count = lax.axis_size(axis)
        ends = count - 1
        head = lax.slice_in_dim(cells, 0, width, axis=dim)
        tail = lax.slice_in_dim(cells, cells.shape[dim] - width, cells.shape[dim], axis=dim)
        cells = jnp.concatenate(
            [
                lax.ppermute(tail, axis, [(i, (i + 1) % count) for i in range(ends)]),
                cells,
                lax.ppermute(head, axis, [((i + 1) % count, i) for i in range(ends)]),
            ],
            axis=dim,
        )
    return cells


def per_device(vectors, left_ops, right_ops, block_sizes, term_shifts):
    block_count = vectors.shape[1]
    block_order = vectors.shape[2]
    row_index = jnp.arange(block_order, dtype=jnp.int32)
    live_mask = (row_index[None, :, None] < block_sizes[:, 0][:, None, None]) & (
        row_index[None, None, :] < block_sizes[:, 1][:, None, None]
    )
    masked = jnp.where(live_mask[None], vectors, jnp.zeros((), vectors.dtype))
    padded = extended(masked, (("bond", 1),), 1)

    def add_term(accumulated, operands):
        left_block, right_block, term_shift = operands
        start_block = 1 - term_shift
        source_blocks = lax.dynamic_slice_in_dim(padded, start_block, block_count, 1)
        half_product = jnp.einsum(
            "bik,vbkj->vbij", left_block, source_blocks, preferred_element_type=jnp.float32
        ).astype(jnp.bfloat16)
        term_value = jnp.einsum(
            "vbij,blj->vbil", half_product, right_block, preferred_element_type=jnp.float32
        )
        return (accumulated + term_value, None)

    initial = jnp.zeros((vectors.shape[0], block_count, block_order, block_order), jnp.float32)
    accumulated, _ = lax.scan(add_term, initial, (left_ops, right_ops, term_shifts))
    op_count = lax.axis_size("op")
    share_rows = block_order // op_count
    first_row = lax.axis_index("op") * share_rows
    summed = lax.psum(accumulated, "op")
    own_share = lax.dynamic_slice_in_dim(summed, first_row, share_rows, 2)
    live_share = lax.dynamic_slice_in_dim(live_mask, first_row, share_rows, 1)
    return jnp.where(live_share[None], own_share, jnp.zeros((), own_share.dtype))


def solution(mesh):
    in_specs = (
        P(None, "bond", None, None),
        P("op", "bond", None, None),
        P("op", "bond", None, None),
        P("bond", None),
        P("op"),
    )
    out_specs = P(None, "bond", "op", None)
    return jax.shard_map(
        per_device, mesh=mesh, in_specs=in_specs, out_specs=out_specs, check_vma=False
    )
```

profile of v0, /device:TPU:2, one launch (start us, length us, event | category | flops | bytes accessed | tf_op | source)
XLA Modules:
  0.0 213.6 jit_solution(7319213809346613324)
XLA Ops:
  6.5 0.0 all-reduce.2.cloned.1.call-start
  6.5 1.0 slice_reduce_fusion.1
  7.5 0.1 iota_compare_fusion
  7.6 0.1 broadcast_and_fusion
  7.7 0.0 copy-start
  7.7 1.1 broadcast_select_fusion
  8.9 1.9 collective-permute-start
  10.8 3.6 %collective-permute-start.1 = (bf16[2,1,256,256]{3,2,1,0:T(8,128)(2,1)S(1)}, bf16[2,1,256,256]{3,2,1,0:T(8,128)(2,1)S(1)}, u32[]{:S(2)}, u32[]{:S(2)}) collective-permute-start(bf16[2,1,256,256]{3,2,1,0:T(8,128)(2,1)S(1)} %get-tuple-element.119), channel_id=1, source_target_pairs={{1,0},{2,1},{3,2},{4,3},{5,4},{6,5},{7,6},{8,7},{9,8},{10,9},{11,1... | collective-permute-start | bytes 786440 | tf_op jit(solution)/shard_map/ppermute | solution.py:17
  14.5 2.1 collective-permute-done
  16.6 1.8 collective-permute-done.1
  18.3 0.1 pad_maximum_fusion
  18.5 0.0 copy-done
  18.5 29.0 %while.13 = (s32[]{:T(128)}, f32[2,2,256,256]{2,3,0,1:T(8,128)S(1)}, bf16[8,2,256,256]{3,2,1,0:T(8,128)(2,1)}, s32[8]{0:T(128)S(1)}, bf16[2,4,256,256]{3,2,1,0:T...) while((s32[]{:T(128)}, ...), condition=%wide.region_1.2_spmd.clone, body=%wide.region_0.1_spmd.clone.sunk | while | flops 269221888 | bytes 3147952 | solution.py:47
  18.5 0.7 dynamic_slice.60
  20.4 1.7 fusion.20
  22.1 0.7 dynamic_slice.60
  24.0 1.7 fusion.20
  25.7 0.7 dynamic_slice.60
  27.7 1.7 fusion.20
  29.4 0.7 dynamic_slice.60
  31.3 1.7 fusion.20
  33.0 0.7 dynamic_slice.60
  34.9 1.7 fusion.20
  36.6 0.7 dynamic_slice.60
  38.5 1.7 fusion.20
  40.2 0.7 dynamic_slice.60
  42.2 1.7 fusion.20
  43.9 0.7 dynamic_slice.60
  45.8 1.7 fusion.20
  47.5 1.4 copy.6
  48.9 0.0 all-reduce.2.cloned.1.call-update
  48.9 156.4 %all-reduce.2.cloned.1.call-done = f32[2,2,256,256]{3,2,1,0:T(8,128)} async-done(((f32[2,2,256,256]{3,2,1,0:T(8,128)}), f32[2,2,256,256]{3,2,1,0:T(8,128)}) %all-reduce.2.cloned.1.call-update) | async-done | bytes 1048592 | tf_op jit(solution)/shard_map/psum | solution.py:51
  205.3 1.5 dynamic-slice_select_fusion
  (3 shorter events, 0.0 us)
Async XLA Ops:
  6.5 198.7 %all-reduce.2.cloned.1.call-start = ((), (), s32[]{:S(2)}) async-start(), calls=%async_computation | async-start | bytes 2097152 | tf_op jit(solution)/shard_map/psum | solution.py:51
  7.7 10.7 %copy-start = (s32[8]{0:T(128)S(1)}, s32[8]{0:T(128)}, u32[]{:S(2)}) copy-start(s32[8]{0:T(128)} %param.11) | copy-start | bytes 100
  8.9 7.7 %collective-permute-start = (bf16[2,1,256,256]{3,2,1,0:T(8,128)(2,1)S(1)}, bf16[2,1,256,256]{3,2,1,0:T(8,128)(2,1)S(1)}, u32[]{:S(2)}, u32[]{:S(2)}) collective-permute-start(bf16[2,1,256,256]{3,2,1,0:T(8,128)(2,1)S(1)} %get-tuple-element.118), channel_id=1, source_target_pairs={{0,1},{1,2},{2,3},{3,4},{4,5},{5,6},{6,7},{7,8},{8,9},{9,10},{10,1... | collective-permute-start | bytes 786440 | tf_op jit(solution)/shard_map/ppermute | solution.py:15
  10.8 7.5 %collective-permute-start.1 = (bf16[2,1,256,256]{3,2,1,0:T(8,128)(2,1)S(1)}, bf16[2,1,256,256]{3,2,1,0:T(8,128)(2,1)S(1)}, u32[]{:S(2)}, u32[]{:S(2)}) collective-permute-start(bf16[2,1,256,256]{3,2,1,0:T(8,128)(2,1)S(1)} %get-tuple-element.119), channel_id=1, source_target_pairs={{1,0},{2,1},{3,2},{4,3},{5,4},{6,5},{7,6},{8,7},{9,8},{10,9},{11,1... | collective-permute-start | bytes 786440 | tf_op jit(solution)/shard_map/ppermute | solution.py:17
Sparse Core Ops, SparseCore 0:
  49.0 156.2 all-reduce.1
where the time goes:
time: 214 us
  waiting for transfers between devices  160 us (75%)
  between operations  13.5 us (6%)
  matrix products  13.4 us (6%)
  loops' own time  10.4 us (5%)
  local copies, waits for them, and re-layouts  7.58 us (4%)
  starting transfers between devices  5.56 us (3%)
  other arithmetic  2.93 us (1%)
    psum x1, waiting for transfers between devices, per_device(): summed = lax.psum(accumulated, 'op')  156 us
    dot_general x8, matrix products, add_term(): jnp.einsum('vbij,blj->vbil', half_product, right_block, preferred_element...  13.4 us
    another operation x1, loops' own time, per_device(): lax.scan(add_term, initial, (left_ops, right_ops, term_shifts))  10.4 us
    dynamic_slice x8, local copies, waits for them, and re-layouts, per_device(): lax.scan(add_term, initial, (left_ops, right_ops, term_shifts))  5.2 us
  transfers between devices with their start and end apart: 3, of which 3 were waited for; matrix products, arithmetic and copies ran while one was open for 0% of the time, Pallas kernels for 0%

commit v1 on v0

--- a/solution.py
+++ b/solution.py
@@ -48,7 +48,7 @@
     op_count = lax.axis_size("op")
     share_rows = block_order // op_count
     first_row = lax.axis_index("op") * share_rows
-    summed = lax.psum(accumulated, "op")
+    summed = jnp.sum(lax.all_gather(accumulated, "op"), axis=0)
     own_share = lax.dynamic_slice_in_dim(summed, first_row, share_rows, 2)
     live_share = lax.dynamic_slice_in_dim(live_mask, first_row, share_rows, 1)
     return jnp.where(live_share[None], own_share, jnp.zeros((), own_share.dtype))

time: 214 us -> 265 us (1.24)
  the two profiles are of different devices: /device:TPU:2 before, /device:TPU:1 now
where the time goes in v1:
time: 265 us; the launch traced here: 264 us
  waiting for transfers between devices  201 us (76%)
  between operations  13.5 us (5%)
  matrix products  13.4 us (5%)
  starting transfers between devices  10.1 us (4%)
  loops' own time  9.99 us (4%)
  other arithmetic  8.66 us (3%)
  local copies, waits for them, and re-layouts  8.11 us (3%)
    all_gather x1, waiting for transfers between devices, per_device(): summed = jnp.sum(lax.all_gather(accumulated, 'op'), axis=0)  198 us
    dot_general x8, matrix products, add_term(): jnp.einsum('vbij,blj->vbil', half_product, right_block, preferred_element...  13.4 us
    another operation x1, loops' own time, per_device(): lax.scan(add_term, initial, (left_ops, right_ops, term_shifts))  9.99 us
    reduce_sum x1, other arithmetic, per_device(): summed = jnp.sum(lax.all_gather(accumulated, 'op'), axis=0)  6.99 us
    ppermute x1, starting transfers between devices, extended(): lax.ppermute(head, axis, [((i + 1) % count, i) for i in range(ends)])  5.55 us
  transfers between devices with their start and end apart: 3, of which 2 were waited for; matrix products, arithmetic and copies ran while one was open for 0% of the time, Pallas kernels for 0%

profile of v1, /device:TPU:1, one launch (start us, length us, event | category | flops | bytes accessed | tf_op | source)
XLA Modules:
  0.0 264.2 jit_solution(16366737950591451829)
XLA Ops:
  6.5 0.0 all-gather.3.cloned.1.call-start
  6.5 1.0 slice_reduce_fusion.1
  7.5 0.1 iota_compare_fusion
  7.6 0.1 broadcast_and_fusion
  7.7 0.3 copy.6
  8.0 0.0 copy-start.1
  8.0 1.1 broadcast_select_fusion
  9.2 4.5 %collective-permute-start = (bf16[2,1,256,256]{3,2,1,0:T(8,128)(2,1)S(1)}, bf16[2,1,256,256]{3,2,1,0:T(8,128)(2,1)S(1)}, u32[]{:S(2)}, u32[]{:S(2)}) collective-permute-start(bf16[2,1,256,256]{3,2,1,0:T(8,128)(2,1)S(1)} %get-tuple-element.118), channel_id=1, source_target_pairs={{0,1},{1,2},{2,3},{3,4},{4,5},{5,6},{6,7},{7,8},{8,9},{9,10},{10,1... | collective-permute-start | bytes 786440 | tf_op jit(solution)/shard_map/ppermute | solution.py:15
  13.7 5.6 %collective-permute-start.1 = (bf16[2,1,256,256]{3,2,1,0:T(8,128)(2,1)S(1)}, bf16[2,1,256,256]{3,2,1,0:T(8,128)(2,1)S(1)}, u32[]{:S(2)}, u32[]{:S(2)}) collective-permute-start(bf16[2,1,256,256]{3,2,1,0:T(8,128)(2,1)S(1)} %get-tuple-element.119), channel_id=1, source_target_pairs={{1,0},{2,1},{3,2},{4,3},{5,4},{6,5},{7,6},{8,7},{9,8},{10,9},{11,1... | collective-permute-start | bytes 786440 | tf_op jit(solution)/shard_map/ppermute | solution.py:17
  19.2 0.0 collective-permute-done
  19.3 2.1 collective-permute-done.1
  21.4 0.1 pad_maximum_fusion
  21.5 0.0 copy-done.1
  21.5 28.4 %while.13 = (s32[]{:T(128)}, f32[2,2,256,256]{2,3,0,1:T(8,128)S(1)}, bf16[8,2,256,256]{3,2,1,0:T(8,128)(2,1)}, s32[8]{0:T(128)S(1)}, bf16[2,4,256,256]{3,2,1,0:T...) while((s32[]{:T(128)}, ...), condition=%wide.region_1.2_spmd.clone, body=%wide.region_0.1_spmd.clone.sunk | while | flops 269221888 | bytes 3147952 | solution.py:47
  21.5 0.6 dynamic_slice.60
  23.4 1.7 fusion.20
  25.1 0.6 dynamic_slice.60
  26.9 1.7 fusion.20
  28.6 0.6 dynamic_slice.60
  30.4 1.7 fusion.20
  32.1 0.6 dynamic_slice.60
  34.0 1.7 fusion.20
  35.7 0.6 dynamic_slice.60
  37.5 1.7 fusion.20
  39.2 0.6 dynamic_slice.60
  41.1 1.7 fusion.20
  42.8 0.6 dynamic_slice.60
  44.6 1.7 fusion.20
  46.3 0.6 dynamic_slice.60
  48.2 1.7 fusion.20
  49.9 0.0 copy-start
  49.9 1.0 copy-done
  50.8 0.0 all-gather.3.cloned.1.call-update
  50.9 0.1 constant_dynamic-slice_fusion.1
  51.0 198.4 %all-gather.3.cloned.1.call-done = f32[32,2,256,256]{2,3,0,1:T(8,128)} async-done(((f32[2,2,256,256]{2,3,0,1:T(8,128)}), f32[32,2,256,256]{2,3,0,1:T(8,128)}) %all-gather.3.cloned.1.call-update) | async-done | bytes 16777232 | tf_op jit(solution)/shard_map/all_gather | solution.py:51
  249.4 7.0 %reduce_sum.9 = f32[2,2,256,256]{2,3,0,1:T(8,128)S(1)} reduce(f32[16,2,2,256,256]{3,4,1,0,2:T(8,128)} %bitcast.36, f32[]{:T(128)} %constant.42.clone.1), dimensions={0}, to_apply=%region_2.3 | reduce | flops 3932160 | bytes 17825796 | tf_op jit(solution)/shard_map/reduce_sum | solution.py:51
  256.4 0.2 dynamic-slice_select_fusion
  256.6 0.8 copy.7
  (2 shorter events, 0.0 us)
Async XLA Ops:
  6.5 242.9 %all-gather.3.cloned.1.call-start = ((), (), s32[]{:S(2)}) async-start(), calls=%async_computation | async-start | bytes 17825792 | tf_op jit(solution)/shard_map/all_gather | solution.py:51
  8.0 13.5 %copy-start.1 = (s32[8]{0:T(128)S(1)}, s32[8]{0:T(128)}, u32[]{:S(2)}) copy-start(s32[8]{0:T(128)} %param.11) | copy-start | bytes 100
  9.2 10.1 %collective-permute-start = (bf16[2,1,256,256]{3,2,1,0:T(8,128)(2,1)S(1)}, bf16[2,1,256,256]{3,2,1,0:T(8,128)(2,1)S(1)}, u32[]{:S(2)}, u32[]{:S(2)}) collective-permute-start(bf16[2,1,256,256]{3,2,1,0:T(8,128)(2,1)S(1)} %get-tuple-element.118), channel_id=1, source_target_pairs={{0,1},{1,2},{2,3},{3,4},{4,5},{5,6},{6,7},{7,8},{8,9},{9,10},{10,1... | collective-permute-start | bytes 786440 | tf_op jit(solution)/shard_map/ppermute | solution.py:15
  13.7 7.7 %collective-permute-start.1 = (bf16[2,1,256,256]{3,2,1,0:T(8,128)(2,1)S(1)}, bf16[2,1,256,256]{3,2,1,0:T(8,128)(2,1)S(1)}, u32[]{:S(2)}, u32[]{:S(2)}) collective-permute-start(bf16[2,1,256,256]{3,2,1,0:T(8,128)(2,1)S(1)} %get-tuple-element.119), channel_id=1, source_target_pairs={{1,0},{2,1},{3,2},{4,3},{5,4},{6,5},{7,6},{8,7},{9,8},{10,9},{11,1... | collective-permute-start | bytes 786440 | tf_op jit(solution)/shard_map/ppermute | solution.py:17
  49.9 1.0 copy-start
Sparse Core Ops, SparseCore 0:
  51.0 198.3 all-gather.2
